TPU v7x, 32 devices: a whole 2x2x4 slice. The times are simulated.
32 devices in a mesh: seq: 8 (over z, x), tp: 4 (over y, core).
Axes of the slice: x: 2, y: 2, z: 4, core: 2. Of those that a mesh axis runs over, the one named last changes fastest.
Arguments:
- queries: bfloat16 [1024, 4096], P('seq', 'tp'), may hold values from -600 to 600
- suffix_keys: bfloat16 [1024, 1024], P('seq', 'tp'), may hold values from -6 to 6
- suffix_values: bfloat16 [1024, 1024], P('seq', 'tp'), may hold values from -6 to 6
- prefix_keys: bfloat16 [512, 1024], P('seq', 'tp'), may hold values from -6 to 6
- prefix_values: bfloat16 [512, 1024], P('seq', 'tp'), may hold values from -6 to 6
- suffix_lengths: int32 [24], replicated, may hold values from 1 to 128, 1024 in all
- request_group: int32 [24], replicated, may hold values from 0 to 3
- block_group: int32 [8], replicated, may hold values from 0 to 3, as said below
Outputs:
- attended: bfloat16 [1024, 4096], P('seq', 'tp')
- cache_keys: bfloat16 [1024, 1024], P(('seq', 'tp'))
- cache_values: bfloat16 [1024, 1024], P(('seq', 'tp'))
Inputs may be any that keep to these rules, and one draw needn't show every extreme that they name: `suffix_lengths`: the suffixes fill the 1024 packed tokens end to end in order; the longest has exactly 128 tokens. `block_group`: each prefix is held by exactly 2 blocks, in any order.
All inputs are finite; a program needn't handle non-finite values.
Results may differ from a plain program's by a relative error of at most 0.009.
The roundings to bfloat16 on the way count: a program that leaves them out, or rounds other values in their place, can miss the bound.
Values may be sent and summed in bfloat16 or wider, within the bound.
No kernel may reach another device: no remote copies, remote signals or barrier semaphores. Data moves between devices by JAX's collectives and lax.ppermute only.
A program may use at most 64 MiB of HBM per device.

v0:
```python
import math
import jax
import jax.numpy as jnp
from jax import lax
from jax.sharding import PartitionSpec as P

HD = 128
GROUPS = 4
BIG_NEGATIVE = -1e30


def from_behind(array, axis, by):
    length = lax.axis_size(axis)
    pairs = [(i, i + by) for i in range(length) if 0 <= i + by < length]
    return lax.ppermute(array, axis, pairs)


def rotate(values, position):
    half = values.shape[-1] // 2
    freq = jnp.exp(
        jnp.arange(half, dtype=jnp.float32) * (-2.0 * math.log(500000.0) / values.shape[-1])
    )
    angle = position.astype(jnp.float32)[:, None] * freq[None, :]
    cosine = jnp.cos(angle)[:, None, :]
    sine = jnp.sin(angle)[:, None, :]
    floats = values.astype(jnp.float32)
    lower = floats[..., :half]
    upper = floats[..., half:]
    return jnp.concatenate(
        [lower * cosine - upper * sine, upper * cosine + lower * sine], axis=-1
    ).astype(jnp.bfloat16)


def token_info(index, suffix_lengths, request_group):
    ends = jnp.cumsum(suffix_lengths)
    request = jnp.sum((index[:, None] >= ends[None, :]).astype(jnp.int32), axis=1)
    onehot = request[:, None] == jnp.arange(suffix_lengths.shape[0], dtype=jnp.int32)[None, :]
    first = jnp.sum(jnp.where(onehot, (ends - suffix_lengths)[None, :], 0), axis=1)
    group = jnp.sum(jnp.where(onehot, request_group[None, :], 0), axis=1)
    return (request, index - first, group)


def body(
    queries,
    suffix_keys,
    suffix_values,
    prefix_keys,
    prefix_values,
    suffix_lengths,
    request_group,
    block_group,
):
    rows = queries.shape[0]
    kv_cols = suffix_keys.shape[1]
    kv_heads = kv_cols // HD
    q_heads = queries.shape[1] // HD
    repeat = q_heads // kv_heads
    devices = lax.axis_size("seq")
    me = lax.axis_index("seq")
    block_rows = prefix_keys.shape[0]
    prefix_len = block_rows * devices // GROUPS
    span = max(1, min(2048 // rows, devices // 8))
    scale = HD ** (-0.5)
    index = me * rows + jnp.arange(rows, dtype=jnp.int32)
    request, offset, group = token_info(index, suffix_lengths, request_group)
    position = offset + prefix_len
    q_rot = rotate(queries.reshape(rows, q_heads, HD), position).reshape(rows, kv_heads, repeat, HD)
    k_rot = rotate(suffix_keys.reshape(rows, kv_heads, HD), position).reshape(rows, kv_cols)

    def update(carry, keys, values, visible):
        high, total, accum = carry
        keys_split = keys.reshape(keys.shape[0], kv_heads, HD)
        values_split = values.reshape(values.shape[0], kv_heads, HD)
        scores = (
            jnp.einsum("bgrd,kgd->bgrk", q_rot, keys_split, preferred_element_type=jnp.float32)
            * scale
        )
        mask = visible[:, None, None, :]
        scores = jnp.where(mask, scores, BIG_NEGATIVE)
        new_high = jnp.maximum(high, jnp.max(scores, axis=-1))
        weights = jnp.where(mask, jnp.exp(scores - new_high[..., None]), 0.0)
        factor = jnp.exp(high - new_high)
        total = total * factor + jnp.sum(weights, axis=-1)
        accum = accum * factor[..., None] + jnp.einsum(
            "bgrk,kgd->bgrd",
            weights.astype(jnp.bfloat16),
            values_split,
            preferred_element_type=jnp.float32,
        )
        return (new_high, total, accum)

    def guarded(carry, keys, values, visible):
        return update(carry, keys, values, visible)

    def suffix_visible(back):
        key_index = (me - back) * rows + jnp.arange(rows, dtype=jnp.int32)
        key_request, _, _ = token_info(key_index, suffix_lengths, request_group)
        return (
            (key_index[None, :] >= 0)
            & (key_request[None, :] == request[:, None])
            & (key_index[None, :] <= index[:, None])
        )

    start_state = (
        jnp.full((rows, kv_heads, repeat), BIG_NEGATIVE, jnp.float32),
        jnp.zeros((rows, kv_heads, repeat), jnp.float32),
        jnp.zeros((rows, kv_heads, repeat, HD), jnp.float32),
    )
    carry = start_state
    keys = lax.all_gather(prefix_keys, "seq", axis=0, tiled=True)
    values = lax.all_gather(prefix_values, "seq", axis=0, tiled=True)
    count = keys.shape[0]
    width = 512

    def one_step(state, step):
        first = step * width
        keys_part = lax.dynamic_slice_in_dim(keys, first, width, 0)
        values_part = lax.dynamic_slice_in_dim(values, first, width, 0)
        row_index = first + jnp.arange(width, dtype=jnp.int32)
        holder = row_index // block_rows
        matches = holder[:, None] == jnp.arange(block_group.shape[0], dtype=jnp.int32)[None, :]
        row_group = jnp.sum(jnp.where(matches, block_group[None, :], 0), axis=1)
        visible = row_group[None, :] == group[:, None]
        return (guarded(state, keys_part, values_part, visible), None)

    carry, _ = lax.scan(one_step, carry, jnp.arange(count // width, dtype=jnp.int32))
    carry = guarded(carry, k_rot, suffix_values, suffix_visible(0))
    for back in range(1, span + 1):
        earlier_keys, earlier_values = from_behind((k_rot, suffix_values), "seq", back)
        carry = guarded(carry, earlier_keys, earlier_values, suffix_visible(back))
    high, total, accum = carry
    attended = (accum / total[..., None]).reshape(rows, q_heads * HD).astype(jnp.bfloat16)
    cache_keys, cache_values = (
        lax.all_to_all(k_rot, "tp", split_axis=0, concat_axis=1, tiled=True),
        lax.all_to_all(suffix_values, "tp", split_axis=0, concat_axis=1, tiled=True),
    )
    return (attended, cache_keys, cache_values)


def solution(mesh):
    return jax.shard_map(
        body,
        mesh=mesh,
        in_specs=(
            P("seq", "tp"),
            P("seq", "tp"),
            P("seq", "tp"),
            P("seq", "tp"),
            P("seq", "tp"),
            P(),
            P(),
            P(),
        ),
        out_specs=(P("seq", "tp"), P(("seq", "tp"), None), P(("seq", "tp"), None)),
        check_vma=False,
    )
```

profile of v0, /device:TPU:0, one launch (start us, length us, event | category | flops | bytes accessed | tf_op | source)
XLA Modules:
  0.0 101.6 jit_solution(3033059807300362979)
XLA Ops:
  0.7 0.8 copy.95
  1.6 0.7 sub.87
  2.4 0.7 select_reduce_fusion.2
  3.1 0.9 copy.101
  4.3 0.3 multiply_cosine_fusion
  4.7 0.7 copy.106
  5.5 5.5 %collective-permute-start = (bf16[128,256]{0,1:T(8,128)(2,1)}, bf16[128,256]{0,1:T(8,128)(2,1)}, u32[]{:S(2)}, u32[]{:S(2)}) collective-permute-start(bf16[128,256]{0,1:T(8,128)(2,1)} %bitcast.19), channel_id=1, source_target_pairs={{0,4},{4,8},{8,12},{12,16},{16,20},{20,24},{24,28},{1,5},{5,9},{9,... | collective-permute-start | bytes 196616 | tf_op jit(solution)/shard_map/ppermute | solution.py:15
  10.9 3.5 %collective-permute-start.1 = (bf16[128,256]{1,0:T(8,128)(2,1)}, bf16[128,256]{1,0:T(8,128)(2,1)}, u32[]{:S(2)}, u32[]{:S(2)}) collective-permute-start(bf16[128,256]{1,0:T(8,128)(2,1)} %param.10), channel_id=1, source_target_pairs={{0,4},{4,8},{8,12},{12,16},{16,20},{20,24},{24,28},{1,5},{5,9},{9,... | collective-permute-start | bytes 196616 | tf_op jit(solution)/shard_map/ppermute | solution.py:15
  14.5 0.7 convert_element_type.70
  15.2 3.3 %all-to-all-start = ((bf16[4,32,256]{2,1,0:T(8,128)(2,1)}), bf16[4,32,256]{2,1,0:T(8,128)(2,1)S(1)}, u32[]{:S(2)}, u32[]{:S(2)}) async-start(bf16[4,32,256]{2,1,0:T(8,128)(2,1)} %convert_element_type.70), calls=%async_computation | async-start | bytes 131072 | tf_op jit(solution)/shard_map/all_to_all | solution.py:134
  18.7 0.2 fusion.46
  18.9 31.0 %all_gather.6 = bf16[512,256]{1,0:T(8,128)(2,1)S(1)} all-gather(bf16[64,256]{1,0:T(8,128)(2,1)S(1)} %copy-done.7), channel_id=1, replica_groups=mesh['seq'=8,'tp'=4] {'seq'}, dimensions={0}, use_global_device_ids=true | all-gather | bytes 294912 | tf_op jit(solution)/shard_map/all_gather | solution.py:110
  49.8 0.1 copy.98
  50.0 0.2 subtract_convert_fusion
  50.4 0.8 compare_and_fusion
  51.2 1.2 %bitcast_reduce_fusion = (f32[128,2,4]{0,2,1:T(4,128)}, f32[2,128,4,512]{3,1,2,0:T(8,128)S(1)}) fusion(pred[128,512]{1,0:T(8,128)(4,1)S(1)} %broadcast_compare_fusion, bf16[512,2,128,1]{0,2,3,1:T(8,128)(2,1)S(1)} %bitcast.101, bf16[128,2,4,64]{3,0,2,1:T(8,128)(2,1)S(1)} %bitcast.98, bf16[128,2,4,64]{3,0,2,1:T(8,128)(2,1)S(1)} %bitcast.95), kind=kOutput, calls=%fused_computation.1 | convolution fusion | flops 136313856 | bytes 2691072 | tf_op jit(solution)/shard_map/while/body/eval_jaxpr/bgrd,kgd->bgrk/dot_general | solution.py:75
  52.4 0.9 fusion.49
  53.3 0.6 copy-done.4
  53.9 3.9 %all-to-all-start.1 = ((bf16[4,32,256]{2,1,0:T(8,128)(2,1)}), bf16[4,32,256]{2,1,0:T(8,128)(2,1)}, u32[]{:S(2)}, u32[]{:S(2)}) async-start(bf16[4,32,256]{2,1,0:T(8,128)(2,1)} %bitcast.29), calls=%async_computation.1 | async-start | bytes 131072 | tf_op jit(solution)/shard_map/all_to_all | solution.py:135
  57.8 31.0 %all_gather.7 = bf16[512,256]{1,0:T(8,128)(2,1)S(1)} all-gather(bf16[64,256]{1,0:T(8,128)(2,1)} %param.12), channel_id=1, replica_groups=mesh['seq'=8,'tp'=4] {'seq'}, dimensions={0}, use_global_device_ids=true | all-gather | bytes 294912 | tf_op jit(solution)/shard_map/all_gather | solution.py:111
  88.9 0.9 copy.124
  89.8 0.8 copy.100
  90.7 1.5 %copy.131 = bf16[4,4,8,256]{3,2,0,1:T(8,128)(2,1)} copy(bf16[4,4,8,256]{3,2,1,0:T(8,128)(2,1)} %bitcast.106) | data formatting | bytes 131072 | tf_op jit(solution)/shard_map/all_to_all | solution.py:134
  92.2 1.5 %copy.132 = bf16[4,4,8,256]{3,2,0,1:T(8,128)(2,1)} copy(bf16[4,4,8,256]{3,2,1,0:T(8,128)(2,1)} %bitcast.46) | data formatting | bytes 131072 | tf_op jit(solution)/shard_map/all_to_all | solution.py:135
  93.6 1.2 %fusion.48 = (f32[128,2,4]{0,2,1:T(4,128)S(1)}, f32[128,2,4,128]{0,3,2,1:T(8,128)S(1)}) fusion(bf16[128,2,128,1]{0,2,3,1:T(8,128)(2,1)} %bitcast.39, bf16[128,2,4,64]{3,0,2,1:T(8,128)(2,1)S(1)} %bitcast.100, bf16[128,2,4,64]{3,0,2,1:T(8,128)(2,1)S(1)} %bitcast.97, pred[128,128]{0,1:T(8,128)(4,1)} %get-tuple-element.67), kind=kOutput, calls=%fused_computation.88 | convolution fusion | flops 34470912 | bytes 872448 | tf_op jit(solution)/shard_map/bgrd,kgd->bgrk/dot_general | solution.py:75
  94.9 0.7 fusion.44
  95.7 0.2 convolution_bitcast_fusion.1
  96.0 0.7 fusion.2
  96.9 1.6 %fusion.7 = f32[128,2,4,128]{0,3,2,1:T(8,128)} fusion(f32[128,2,4,128]{0,3,2,1:T(8,128)S(1)} %convolution_bitcast_fusion.1, bf16[512,2,128,1]{0,2,3,1:T(8,128)(2,1)S(1)} %bitcast.104, f32[2,128,4,512]{3,1,2,0:T(8,128)S(1)} %get-tuple-element.76, f32[128,2,4]{0,2,1:T(4,128)S(1)} %get-tuple-element.66, pred[128,512]{1,0:T(8,128)(4,1)S(1)} %broadcast_compare_fusion, ...), kind=kOutput, calls=%fused_computation.13 | convolution fusion | flops 137363456 | bytes 3489792 | tf_op jit(solution)/shard_map/while/body/eval_jaxpr/bgrk,kgd->bgrd/dot_general | solution.py:84
  98.5 0.9 copy.108
  99.4 1.3 %fusion.14 = bf16[128,2,4,128]{0,3,2,1:T(8,128)(2,1)S(1)} fusion(f32[128,2,4,128]{0,3,2,1:T(8,128)} %fusion.7, bf16[128,2,128,1]{0,2,3,1:T(8,128)(2,1)S(1)} %bitcast.109, f32[128,2,4,128]{0,3,2,1:T(8,128)S(1)} %copy-done.1, f32[128,2,4]{0,2,1:T(4,128)S(1)} %get-tuple-element.52, f32[128,2,4]{0,2,1:T(4,128)S(1)} %get-tuple-element.55, ...), kind=kOutput, calls=%fused_computation.22 | convolution fusion | flops 34340864 | bytes 1400832 | tf_op jit(solution)/shard_map/bgrk,kgd->bgrd/dot_general | solution.py:84
  100.7 0.9 copy.113
  (42 shorter events, 1.3 us)
Async XLA Ops:
  0.6 17.9 %copy-start.2 = (bf16[128,1024]{1,0:T(8,128)(2,1)S(1)}, bf16[128,1024]{1,0:T(8,128)(2,1)}, u32[]{:S(2)}) copy-start(bf16[128,1024]{1,0:T(8,128)(2,1)} %param.8) | copy-start | bytes 786436
  5.5 88.2 %collective-permute-start = (bf16[128,256]{0,1:T(8,128)(2,1)}, bf16[128,256]{0,1:T(8,128)(2,1)}, u32[]{:S(2)}, u32[]{:S(2)}) collective-permute-start(bf16[128,256]{0,1:T(8,128)(2,1)} %bitcast.19), channel_id=1, source_target_pairs={{0,4},{4,8},{8,12},{12,16},{16,20},{20,24},{24,28},{1,5},{5,9},{9,... | collective-permute-start | bytes 196616 | tf_op jit(solution)/shard_map/ppermute | solution.py:15
  10.9 87.5 %collective-permute-start.1 = (bf16[128,256]{1,0:T(8,128)(2,1)}, bf16[128,256]{1,0:T(8,128)(2,1)}, u32[]{:S(2)}, u32[]{:S(2)}) collective-permute-start(bf16[128,256]{1,0:T(8,128)(2,1)} %param.10), channel_id=1, source_target_pairs={{0,4},{4,8},{8,12},{12,16},{16,20},{20,24},{24,28},{1,5},{5,9},{9,... | collective-permute-start | bytes 196616 | tf_op jit(solution)/shard_map/ppermute | solution.py:15
  14.5 4.4 %copy-start.7 = (bf16[64,256]{1,0:T(8,128)(2,1)S(1)}, bf16[64,256]{1,0:T(8,128)(2,1)}, u32[]{:S(2)}) copy-start(bf16[64,256]{1,0:T(8,128)(2,1)} %param.11) | copy-start | bytes 98308
  15.2 38.1 %all-to-all-start = ((bf16[4,32,256]{2,1,0:T(8,128)(2,1)}), bf16[4,32,256]{2,1,0:T(8,128)(2,1)S(1)}, u32[]{:S(2)}, u32[]{:S(2)}) async-start(bf16[4,32,256]{2,1,0:T(8,128)(2,1)} %convert_element_type.70), calls=%async_computation | async-start | bytes 131072 | tf_op jit(solution)/shard_map/all_to_all | solution.py:134
  18.6 31.6 %copy-start.8 = (s32[8]{0:T(128)S(1)}, s32[8]{0:T(128)}, u32[]{:S(2)}) copy-start(s32[8]{0:T(128)} %param.15) | copy-start | bytes 100
  53.3 0.6 copy-start.4
  53.9 38.2 %all-to-all-start.1 = ((bf16[4,32,256]{2,1,0:T(8,128)(2,1)}), bf16[4,32,256]{2,1,0:T(8,128)(2,1)}, u32[]{:S(2)}, u32[]{:S(2)}) async-start(bf16[4,32,256]{2,1,0:T(8,128)(2,1)} %bitcast.29), calls=%async_computation.1 | async-start | bytes 131072 | tf_op jit(solution)/shard_map/all_to_all | solution.py:135
  94.9 2.0 %copy-start = (f32[128,2,4,128]{0,3,2,1:T(8,128)}, f32[128,2,4,128]{0,3,2,1:T(8,128)S(1)}, u32[]{:S(2)}) copy-start(f32[128,2,4,128]{0,3,2,1:T(8,128)S(1)} %get-tuple-element.72) | copy-start | bytes 1572868
  94.9 1.8 %copy-start.5 = (pred[128,128]{0,1:T(8,128)(4,1)S(1)}, pred[128,128]{0,1:T(8,128)(4,1)}, u32[]{:S(2)}) copy-start(pred[128,128]{0,1:T(8,128)(4,1)} %get-tuple-element.67) | copy-start | bytes 49156
  95.7 1.1 %copy-start.6 = (f32[128,2,4]{0,2,1:T(4,128)S(1)}, f32[128,2,4]{0,2,1:T(4,128)}, u32[]{:S(2)}) copy-start(f32[128,2,4]{0,2,1:T(4,128)} %get-tuple-element.75) | copy-start | bytes 12292
  95.7 1.1 %copy-start.3 = (bf16[512,256]{0,1:T(8,128)(2,1)S(1)}, bf16[512,256]{0,1:T(8,128)(2,1)}, u32[]{:S(2)}) copy-start(bf16[512,256]{0,1:T(8,128)(2,1)} %copy.100) | copy-start | bytes 786436
  96.9 2.6 %copy-start.1 = (f32[128,2,4,128]{0,3,2,1:T(8,128)S(1)}, f32[128,2,4,128]{0,3,2,1:T(8,128)}, u32[]{:S(2)}) copy-start(f32[128,2,4,128]{0,3,2,1:T(8,128)} %copy-done) | copy-start | bytes 1572868
where the time goes:
time: 102 us
  blocking collectives  62 us (61%)
  starting transfers between devices  16.1 us (16%)
  local copies, waits for them, and re-layouts  11.1 us (11%)
  matrix products  6.46 us (6%)
  other arithmetic  5.01 us (5%)
    all_gather x1, blocking collectives, body(): values = lax.all_gather(prefix_values, 'seq', axis=0, tiled=True)  31 us
    all_gather x1, blocking collectives, body(): keys = lax.all_gather(prefix_keys, 'seq', axis=0, tiled=True)  31 us
    ppermute x2, starting transfers between devices, from_behind(): return lax.ppermute(array, axis, pairs)  8.92 us
    all_to_all x1, starting transfers between devices, body(): lax.all_to_all(suffix_values, 'tp', split_axis=0, concat_axis=1, tiled=True)  3.89 us
    dot_general x3, matrix products, update(): jnp.einsum('bgrd,kgd->bgrk', q_rot, keys_split, preferred_element_type=jn...  3.34 us
    all_to_all x1, starting transfers between devices, body(): lax.all_to_all(k_rot, 'tp', split_axis=0, concat_axis=1, tiled=True)  3.28 us
    dot_general x3, matrix products, update(): jnp.einsum('bgrk,kgd->bgrd', weights.astype(jnp.bfloat16), values_split,...  3.12 us
    unnamed x23, local copies, waits for them, and re-layouts  2.76 us
  transfers between devices with their start and end apart: 4, of which 0 were waited for; matrix products, arithmetic and copies ran while one was open for 14% of the time, Pallas kernels for 0%

commit v1 on v0

--- a/solution.py
+++ b/solution.py
@@ -107,7 +107,12 @@
         jnp.zeros((rows, kv_heads, repeat, HD), jnp.float32),
     )
     carry = start_state
-    keys = lax.all_gather(prefix_keys, "seq", axis=0, tiled=True)
+    ring = [prefix_keys]
+    for hop in range(7):
+        ring.append(lax.ppermute(ring[-1], "seq", [(dev, (dev + 1) % 8) for dev in range(8)]))
+    keys = jnp.roll(
+        jnp.concatenate(ring[::-1], axis=0), (lax.axis_index("seq") + 1) * ring[0].shape[0], axis=0
+    )
     values = lax.all_gather(prefix_values, "seq", axis=0, tiled=True)
     count = keys.shape[0]
     width = 512

time: 102 us -> 96.5 us (0.946)
  blocking collectives: 62 us -> 30.7 us
  waiting for transfers between devices: 0.01 us -> 30.4 us
  matrix products: 6.46 us -> 2.42 us
  starting transfers between devices: 16.1 us -> 20 us
  local copies, waits for them, and re-layouts: 11.1 us -> 7.97 us
  other arithmetic: 5.01 us -> 3.54 us
    all_gather x1 -> x0, blocking collectives: 31 us -> none  [body(): keys = lax.all_gather(prefix_keys, 'seq', axis=0, tiled=True)]
    ppermute x0 -> x7, waiting for transfers between devices: none -> 30.4 us  [body(): lax.ppermute(ring[-1], 'seq', [(dev, (dev + 1) % 8) for dev in range(8)])]
    ppermute x0 -> x7, starting transfers between devices: none -> 6.62 us  [body(): lax.ppermute(ring[-1], 'seq', [(dev, (dev + 1) % 8) for dev in range(8)])]
    dot_general x3, matrix products: 3.34 us -> 1.26 us  [update(): jnp.einsum('bgrd,kgd->bgrk', q_rot, keys_split, preferred_element_type=jn...]
    ppermute x2, starting transfers between devices: 8.92 us -> 6.86 us  [from_behind(): return lax.ppermute(array, axis, pairs)]
    dot_general x3, matrix products: 3.12 us -> 1.16 us  [update(): jnp.einsum('bgrk,kgd->bgrd', weights.astype(jnp.bfloat16), values_split,...]
    unnamed x23 -> x12, local copies, waits for them, and re-layouts: 2.76 us -> 3.02 us
  transfers between devices with their start and end apart: 4 -> 11, of which waited for: 0 -> 5; matrix products, arithmetic and copies ran while one was open for 14% -> 9% of each run, Pallas kernels for 0% -> 0%
where the time goes in v1:
time: 96.5 us; the launch traced here: 96.1 us
  blocking collectives  30.7 us (32%)
  waiting for transfers between devices  30.4 us (32%)
  starting transfers between devices  20 us (21%)
  local copies, waits for them, and re-layouts  7.97 us (8%)
  other arithmetic  3.54 us (4%)
  matrix products  2.42 us (3%)
    all_gather x1, blocking collectives, body(): values = lax.all_gather(prefix_values, 'seq', axis=0, tiled=True)  30.7 us
    ppermute x7, waiting for transfers between devices, body(): lax.ppermute(ring[-1], 'seq', [(dev, (dev + 1) % 8) for dev in range(8)])  30.4 us
    ppermute x2, starting transfers between devices, from_behind(): return lax.ppermute(array, axis, pairs)  6.86 us
    ppermute x7, starting transfers between devices, body(): lax.ppermute(ring[-1], 'seq', [(dev, (dev + 1) % 8) for dev in range(8)])  6.62 us
    all_to_all x1, starting transfers between devices, body(): lax.all_to_all(suffix_values, 'tp', split_axis=0, concat_axis=1, tiled=True)  3.29 us
    all_to_all x1, starting transfers between devices, body(): lax.all_to_all(k_rot, 'tp', split_axis=0, concat_axis=1, tiled=True)  3.28 us
    unnamed x12, local copies, waits for them, and re-layouts  3.02 us
  transfers between devices with their start and end apart: 11, of which 5 were waited for; matrix products, arithmetic and copies ran while one was open for 9% of the time, Pallas kernels for 0%

profile of v1, /device:TPU:0, one launch (start us, length us, event | category | flops | bytes accessed | tf_op | source)
XLA Modules:
  0.0 96.1 jit_solution(17891337581044361013)
XLA Ops:
  0.6 0.9 copy.109
  1.6 3.0 %collective-permute-start = (bf16[64,256]{0,1:T(8,128)(2,1)S(1)}, bf16[64,256]{0,1:T(8,128)(2,1)S(1)}, u32[]{:S(2)}, u32[]{:S(2)}) collective-permute-start(bf16[64,256]{0,1:T(8,128)(2,1)S(1)} %copy.109), channel_id=1, source_target_pairs={{0,4},{4,8},{8,12},{12,16},{16,20},{20,24},{24,28},{28,0},{1,5},{5... | collective-permute-start | bytes 98312 | tf_op jit(solution)/shard_map/ppermute | solution.py:112
  4.6 0.7 copy.108
  5.5 0.7 sub.92
  6.2 0.7 select_reduce_fusion.2
  7.0 0.9 copy.117
  8.1 0.3 multiply_cosine_fusion
  8.7 3.5 %collective-permute-start.7 = (bf16[128,256]{0,1:T(8,128)(2,1)S(1)}, bf16[128,256]{0,1:T(8,128)(2,1)S(1)}, u32[]{:S(2)}, u32[]{:S(2)}) collective-permute-start(bf16[128,256]{0,1:T(8,128)(2,1)S(1)} %bitcast.108), channel_id=1, source_target_pairs={{0,4},{4,8},{8,12},{12,16},{16,20},{20,24},{24,28},{1,5},{5,9},{9,... | collective-permute-start | bytes 196616 | tf_op jit(solution)/shard_map/ppermute | solution.py:15
  12.2 3.4 %collective-permute-start.8 = (bf16[128,256]{1,0:T(8,128)(2,1)}, bf16[128,256]{1,0:T(8,128)(2,1)S(1)}, u32[]{:S(2)}, u32[]{:S(2)}) collective-permute-start(bf16[128,256]{1,0:T(8,128)(2,1)} %param.10), channel_id=1, source_target_pairs={{0,4},{4,8},{8,12},{12,16},{16,20},{20,24},{24,28},{1,5},{5,9},{9,... | collective-permute-start | bytes 196616 | tf_op jit(solution)/shard_map/ppermute | solution.py:15
  15.7 0.7 convert_element_type.70
  16.4 3.3 %all-to-all-start = ((bf16[4,32,256]{2,1,0:T(8,128)(2,1)}), bf16[4,32,256]{2,1,0:T(8,128)(2,1)S(1)}, u32[]{:S(2)}, u32[]{:S(2)}) async-start(bf16[4,32,256]{2,1,0:T(8,128)(2,1)} %convert_element_type.70), calls=%async_computation | async-start | bytes 131072 | tf_op jit(solution)/shard_map/all_to_all | solution.py:139
  20.5 1.6 %collective-permute-start.1 = (bf16[64,256]{0,1:T(8,128)(2,1)S(1)}, bf16[64,256]{0,1:T(8,128)(2,1)S(1)}, u32[]{:S(2)}, u32[]{:S(2)}) collective-permute-start(bf16[64,256]{0,1:T(8,128)(2,1)S(1)} %collective-permute-done), channel_id=1, source_target_pairs={{0,4},{4,8},{8,12},{12,16},{16,20},{20,24},{24,28},{28,0},{1,5},{5... | collective-permute-start | bytes 98312 | tf_op jit(solution)/shard_map/ppermute | solution.py:112
  22.1 0.3 fusion.47
  22.4 5.3 %collective-permute-done.1 = bf16[64,256]{0,1:T(8,128)(2,1)S(1)} collective-permute-done((bf16[64,256]{0,1:T(8,128)(2,1)S(1)}, bf16[64,256]{0,1:T(8,128)(2,1)S(1)}, u32[]{:S(2)}, u32[]{:S(2)}) %collective-permute-start.1) | collective-permute-done | bytes 32800 | tf_op jit(solution)/shard_map/ppermute | solution.py:112
  27.7 7.0 %collective-permute-done.2 = bf16[64,256]{0,1:T(8,128)(2,1)S(1)} collective-permute-done((bf16[64,256]{0,1:T(8,128)(2,1)S(1)}, bf16[64,256]{0,1:T(8,128)(2,1)S(1)}, u32[]{:S(2)}, u32[]{:S(2)}) %collective-permute-start.2) | collective-permute-done | bytes 32800 | tf_op jit(solution)/shard_map/ppermute | solution.py:112
  34.7 6.9 %collective-permute-done.3 = bf16[64,256]{0,1:T(8,128)(2,1)S(1)} collective-permute-done((bf16[64,256]{0,1:T(8,128)(2,1)S(1)}, bf16[64,256]{0,1:T(8,128)(2,1)S(1)}, u32[]{:S(2)}, u32[]{:S(2)}) %collective-permute-start.3) | collective-permute-done | bytes 32800 | tf_op jit(solution)/shard_map/ppermute | solution.py:112
  41.7 6.8 %collective-permute-done.4 = bf16[64,256]{0,1:T(8,128)(2,1)S(1)} collective-permute-done((bf16[64,256]{0,1:T(8,128)(2,1)S(1)}, bf16[64,256]{0,1:T(8,128)(2,1)S(1)}, u32[]{:S(2)}, u32[]{:S(2)}) %collective-permute-start.4) | collective-permute-done | bytes 32800 | tf_op jit(solution)/shard_map/ppermute | solution.py:112
  48.6 3.3 %all-to-all-start.1 = ((bf16[4,32,256]{2,1,0:T(8,128)(2,1)}), bf16[4,32,256]{2,1,0:T(8,128)(2,1)S(1)}, u32[]{:S(2)}, u32[]{:S(2)}) async-start(bf16[4,32,256]{2,1,0:T(8,128)(2,1)} %bitcast.29), calls=%async_computation.1 | async-start | bytes 131072 | tf_op jit(solution)/shard_map/all_to_all | solution.py:140
  51.9 30.7 %all_gather.3 = bf16[512,256]{1,0:T(8,128)(2,1)S(1)} all-gather(bf16[64,256]{1,0:T(8,128)(2,1)S(1)} %copy-done.1), channel_id=1, replica_groups=mesh['seq'=8,'tp'=4] {'seq'}, dimensions={0}, use_global_device_ids=true | all-gather | bytes 294912 | tf_op jit(solution)/shard_map/all_gather | solution.py:116
  82.6 0.9 copy.141
  83.7 0.6 copy.148
  84.4 0.6 copy.149
  85.0 2.0 %collective-permute-start.6 = (bf16[64,256]{0,1:T(8,128)(2,1)S(1)}, bf16[64,256]{0,1:T(8,128)(2,1)S(1)}, u32[]{:S(2)}, u32[]{:S(2)}) collective-permute-start(bf16[64,256]{0,1:T(8,128)(2,1)S(1)} %collective-permute-done.5), channel_id=1, source_target_pairs={{0,4},{4,8},{8,12},{12,16},{16,20},{20,24},{24,28},{28,0},{1,5},{5... | collective-permute-start | bytes 98312 | tf_op jit(solution)/shard_map/ppermute | solution.py:112
  87.0 0.4 fusion.46
  87.5 4.5 %collective-permute-done.6 = bf16[64,256]{0,1:T(8,128)(2,1)S(1)} collective-permute-done((bf16[64,256]{0,1:T(8,128)(2,1)S(1)}, bf16[64,256]{0,1:T(8,128)(2,1)S(1)}, u32[]{:S(2)}, u32[]{:S(2)}) %collective-permute-start.6) | collective-permute-done | bytes 32800 | tf_op jit(solution)/shard_map/ppermute | solution.py:112
  92.0 0.5 concatenate.18
  92.7 0.6 fusion
  93.4 0.2 convolution_bitcast_fusion.1
  93.6 0.5 fusion.1
  94.3 0.7 fusion.6
  95.0 0.3 fusion.13
  95.2 0.9 copy.129
  (45 shorter events, 2.5 us)
Async XLA Ops:
  0.6 19.0 %copy-start = (bf16[128,1024]{1,0:T(8,128)(2,1)S(1)}, bf16[128,1024]{1,0:T(8,128)(2,1)}, u32[]{:S(2)}) copy-start(bf16[128,1024]{1,0:T(8,128)(2,1)} %param.8) | copy-start | bytes 786436
  1.6 18.9 %collective-permute-start = (bf16[64,256]{0,1:T(8,128)(2,1)S(1)}, bf16[64,256]{0,1:T(8,128)(2,1)S(1)}, u32[]{:S(2)}, u32[]{:S(2)}) collective-permute-start(bf16[64,256]{0,1:T(8,128)(2,1)S(1)} %copy.109), channel_id=1, source_target_pairs={{0,4},{4,8},{8,12},{12,16},{16,20},{20,24},{24,28},{28,0},{1,5},{5... | collective-permute-start | bytes 98312 | tf_op jit(solution)/shard_map/ppermute | solution.py:112
  8.7 78.3 %collective-permute-start.7 = (bf16[128,256]{0,1:T(8,128)(2,1)S(1)}, bf16[128,256]{0,1:T(8,128)(2,1)S(1)}, u32[]{:S(2)}, u32[]{:S(2)}) collective-permute-start(bf16[128,256]{0,1:T(8,128)(2,1)S(1)} %bitcast.108), channel_id=1, source_target_pairs={{0,4},{4,8},{8,12},{12,16},{16,20},{20,24},{24,28},{1,5},{5,9},{9,... | collective-permute-start | bytes 196616 | tf_op jit(solution)/shard_map/ppermute | solution.py:15
  12.2 75.2 %collective-permute-start.8 = (bf16[128,256]{1,0:T(8,128)(2,1)}, bf16[128,256]{1,0:T(8,128)(2,1)S(1)}, u32[]{:S(2)}, u32[]{:S(2)}) collective-permute-start(bf16[128,256]{1,0:T(8,128)(2,1)} %param.10), channel_id=1, source_target_pairs={{0,4},{4,8},{8,12},{12,16},{16,20},{20,24},{24,28},{1,5},{5,9},{9,... | collective-permute-start | bytes 196616 | tf_op jit(solution)/shard_map/ppermute | solution.py:15
  16.4 32.2 %all-to-all-start = ((bf16[4,32,256]{2,1,0:T(8,128)(2,1)}), bf16[4,32,256]{2,1,0:T(8,128)(2,1)S(1)}, u32[]{:S(2)}, u32[]{:S(2)}) async-start(bf16[4,32,256]{2,1,0:T(8,128)(2,1)} %convert_element_type.70), calls=%async_computation | async-start | bytes 131072 | tf_op jit(solution)/shard_map/all_to_all | solution.py:139
  19.8 14.8 %copy-start.2 = (s32[8]{0:T(128)S(1)}, s32[8]{0:T(128)}, u32[]{:S(2)}) copy-start(s32[8]{0:T(128)} %param.15) | copy-start | bytes 100
  19.8 32.0 %copy-start.1 = (bf16[64,256]{1,0:T(8,128)(2,1)S(1)}, bf16[64,256]{1,0:T(8,128)(2,1)}, u32[]{:S(2)}) copy-start(bf16[64,256]{1,0:T(8,128)(2,1)} %param.12) | copy-start | bytes 98308
  20.5 7.2 %collective-permute-start.1 = (bf16[64,256]{0,1:T(8,128)(2,1)S(1)}, bf16[64,256]{0,1:T(8,128)(2,1)S(1)}, u32[]{:S(2)}, u32[]{:S(2)}) collective-permute-start(bf16[64,256]{0,1:T(8,128)(2,1)S(1)} %collective-permute-done), channel_id=1, source_target_pairs={{0,4},{4,8},{8,12},{12,16},{16,20},{20,24},{24,28},{28,0},{1,5},{5... | collective-permute-start | bytes 98312 | tf_op jit(solution)/shard_map/ppermute | solution.py:112
  27.7 7.0 %collective-permute-start.2 = (bf16[64,256]{0,1:T(8,128)(2,1)S(1)}, bf16[64,256]{0,1:T(8,128)(2,1)S(1)}, u32[]{:S(2)}, u32[]{:S(2)}) collective-permute-start(bf16[64,256]{0,1:T(8,128)(2,1)S(1)} %collective-permute-done.1), channel_id=1, source_target_pairs={{0,4},{4,8},{8,12},{12,16},{16,20},{20,24},{24,28},{28,0},{1,5},{5... | collective-permute-start | bytes 98312 | tf_op jit(solution)/shard_map/ppermute | solution.py:112
  34.6 7.0 %collective-permute-start.3 = (bf16[64,256]{0,1:T(8,128)(2,1)S(1)}, bf16[64,256]{0,1:T(8,128)(2,1)S(1)}, u32[]{:S(2)}, u32[]{:S(2)}) collective-permute-start(bf16[64,256]{0,1:T(8,128)(2,1)S(1)} %collective-permute-done.2), channel_id=1, source_target_pairs={{0,4},{4,8},{8,12},{12,16},{16,20},{20,24},{24,28},{28,0},{1,5},{5... | collective-permute-start | bytes 98312 | tf_op jit(solution)/shard_map/ppermute | solution.py:112
  41.6 7.0 %collective-permute-start.4 = (bf16[64,256]{0,1:T(8,128)(2,1)S(1)}, bf16[64,256]{0,1:T(8,128)(2,1)S(1)}, u32[]{:S(2)}, u32[]{:S(2)}) collective-permute-start(bf16[64,256]{0,1:T(8,128)(2,1)S(1)} %collective-permute-done.3), channel_id=1, source_target_pairs={{0,4},{4,8},{8,12},{12,16},{16,20},{20,24},{24,28},{28,0},{1,5},{5... | collective-permute-start | bytes 98312 | tf_op jit(solution)/shard_map/ppermute | solution.py:112
  48.6 36.5 %collective-permute-start.5 = (bf16[64,256]{0,1:T(8,128)(2,1)S(1)}, bf16[64,256]{0,1:T(8,128)(2,1)S(1)}, u32[]{:S(2)}, u32[]{:S(2)}) collective-permute-start(bf16[64,256]{0,1:T(8,128)(2,1)S(1)} %collective-permute-done.4), channel_id=1, source_target_pairs={{0,4},{4,8},{8,12},{12,16},{16,20},{20,24},{24,28},{28,0},{1,5},{5... | collective-permute-start | bytes 98312 | tf_op jit(solution)/shard_map/ppermute | solution.py:112
  48.6 35.8 %all-to-all-start.1 = ((bf16[4,32,256]{2,1,0:T(8,128)(2,1)}), bf16[4,32,256]{2,1,0:T(8,128)(2,1)S(1)}, u32[]{:S(2)}, u32[]{:S(2)}) async-start(bf16[4,32,256]{2,1,0:T(8,128)(2,1)} %bitcast.29), calls=%async_computation.1 | async-start | bytes 131072 | tf_op jit(solution)/shard_map/all_to_all | solution.py:140
  85.0 7.0 %collective-permute-start.6 = (bf16[64,256]{0,1:T(8,128)(2,1)S(1)}, bf16[64,256]{0,1:T(8,128)(2,1)S(1)}, u32[]{:S(2)}, u32[]{:S(2)}) collective-permute-start(bf16[64,256]{0,1:T(8,128)(2,1)S(1)} %collective-permute-done.5), channel_id=1, source_target_pairs={{0,4},{4,8},{8,12},{12,16},{16,20},{20,24},{24,28},{28,0},{1,5},{5... | collective-permute-start | bytes 98312 | tf_op jit(solution)/shard_map/ppermute | solution.py:112
